TPU v7x, 512 devices: a whole 4x4x16 slice. The times are simulated.
512 devices in a mesh: dp: 32 (over y, x, core), wide: 16 (over z).
Axes of the slice: x: 4, y: 4, z: 16, core: 2. Of those that a mesh axis runs over, the one named last changes fastest.
Arguments:
- trunk_out: bfloat16 [16384, 1024], P('dp'), may hold values from -6 to 6
- projection: bfloat16 [1024, 4096], P(None, 'wide'), may hold values from -0.1875 to 0.1875
- transform: bfloat16 [4096, 4096], P('wide'), may hold values from -0.125 to 0.125
- block_mask: int32 [32, 32], P('wide'), may hold values from 0 to 1, as said below
- old_index: bfloat16 [16384, 4096], P('dp', 'wide'), may hold values from -6 to 6
- doc_ids: int32 [16384, 4], P('dp'), may hold values from 0 to 16383, as said below
- labels: int32 [16384, 4], P('dp'), may hold values 0 or 1
Outputs:
- new_embed: bfloat16 [16384, 4096], P('dp', 'wide')
- pair_loss: float32 [16384, 4], P('dp')
- trunk_grad: bfloat16 [16384, 4096], P('dp', 'wide')
Inputs may be any that keep to these rules, and one draw needn't show every extreme that they name: `doc_ids`: in each aligned block of 512 rows, no shard id // 512 is named more than 128 times, and one shard is named exactly 128 times. `block_mask`: each block row has 4 to 24 nonzero entries, and some block row has exactly 24.
All inputs are finite; a program needn't handle non-finite values. No bound on the sum of `labels` on one device may be relied on, other than what follows from the above.
Results may differ from a plain program's by a relative error of at most 0.015.
Values may be sent and summed in bfloat16 or wider, within the bound.
No kernel may reach another device: no remote copies, remote signals or barrier semaphores. Data moves between devices by JAX's collectives and lax.ppermute only.
A program may use at most 128 MiB of HBM per device.

v0:
```python
import math
import jax
import jax.numpy as jnp
from jax import lax
from jax.sharding import PartitionSpec as P

E = 4096
K = 4


def local(trunk_out, projection, transform, block_mask, old_index, doc_ids, labels):
    rows = trunk_out.shape[0]
    e_local = transform.shape[0]
    width = transform.shape[1]
    local_blocks, nblocks = block_mask.shape
    side = e_local // local_blocks
    query = jnp.dot(trunk_out, projection, preferred_element_type=jnp.float32).astype(jnp.bfloat16)
    blocks = transform.reshape(local_blocks, side, nblocks, side)
    masked = (blocks * block_mask[:, None, :, None].astype(jnp.bfloat16)).reshape(e_local, width)
    term = jnp.dot(query, masked, preferred_element_type=jnp.float32)
    new = lax.psum_scatter(
        term.astype(jnp.bfloat16), "wide", scatter_dimension=1, tiled=True
    ).astype(jnp.float32)
    flat = doc_ids.reshape(-1)
    whole = lax.all_gather(old_index, "dp", axis=0, tiled=True)
    old_vec = whole[flat].reshape(rows, K, e_local)
    old_wide = old_vec.astype(jnp.float32)
    scale = 1.0 / math.sqrt(E)
    partial_scores = jnp.einsum("re,rke->rk", new, old_wide)
    score = lax.psum(partial_scores, "wide") * scale
    sign = 2.0 * labels.astype(jnp.float32) - 1.0
    pair_loss = jax.nn.softplus(-sign * score)
    dscore = -sign * jax.nn.sigmoid(-sign * score)
    grad_local = (jnp.einsum("rk,rke->re", dscore, old_wide) * scale).astype(jnp.bfloat16)
    grad_full = lax.all_gather(grad_local, "wide", axis=1, tiled=True)
    trunk_grad = lax.dot_general(
        grad_full, masked, (((1,), (1,)), ((), ())), preferred_element_type=jnp.float32
    )
    return (new.astype(jnp.bfloat16), pair_loss, trunk_grad.astype(jnp.bfloat16))


def solution(mesh):
    return jax.shard_map(
        local,
        mesh=mesh,
        in_specs=(
            P("dp", None),
            P(None, "wide"),
            P("wide", None),
            P("wide", None),
            P("dp", "wide"),
            P("dp", None),
            P("dp", None),
        ),
        out_specs=(P("dp", "wide"), P("dp", None), P("dp", "wide")),
        check_vma=False,
    )
```

profile of v0, /device:TPU:2, one launch (start us, length us, event | category | flops | bytes accessed | tf_op | source)
XLA Modules:
  0.0 241.0 jit_solution(8100249756165127333)
XLA Ops:
  8.0 0.0 copy-start
  8.0 0.0 all-gather.3.cloned.1.call-start
  8.1 0.7 all-gather.3.cloned.1.call-update
  8.7 0.0 reduce-scatter.2.cloned.1.call-start
  8.8 0.7 convert_element_type.23
  9.5 0.3 mul.36
  9.8 0.0 copy-done
  9.8 5.8 %convolution_convert_fusion = bf16[512,4096]{1,0:T(8,128)(2,1)} fusion(bf16[512,1024]{1,0:T(8,128)(2,1)S(1)} %copy-done, bf16[1024,256]{1,0:T(8,128)(2,1)} %param.8, bf16[256,4096]{1,0:T(8,128)(2,1)} %param.9, bf16[32,8,32,128]{3,2,1,0:T(8,128)(2,1)S(1)} %bitcast.21), kind=kOutput, calls=%fused_computation.1 | convolution fusion | flops 1345454080 | bytes 9961472 | tf_op jit(solution)/shard_map/dot_general | solution.py:20
  15.7 0.0 copy-start.2
  15.7 0.0 reduce-scatter.2.cloned.1.call-update
  15.7 0.0 all-gather.5.cloned.1.call-start
  15.7 0.6 copy-done.2
  16.4 0.1 copy.10
  16.5 0.2 reshape.45
  16.7 67.9 %all-gather.3.cloned.1.call-done = bf16[16384,256]{1,0:T(8,128)(2,1)} async-done(((bf16[512,256]{1,0:T(8,128)(2,1)}), bf16[16384,256]{1,0:T(8,128)(2,1)}) %all-gather.3.cloned.1.call-update) | async-done | bytes 8388624 | tf_op jit(solution)/shard_map/all_gather | solution.py:25
  84.7 13.0 %gather_fusion = bf16[2048,256]{1,0:T(8,128)(2,1)} fusion(bf16[16384,256]{1,0:T(8,128)(2,1)} %all-gather.3.cloned.1.call-done, s32[2048]{0:T(1024)S(1)} %broadcast_clamp_fusion), kind=kCustom, calls=%fused_computation | custom fusion | bytes 2105344 | tf_op jit(solution)/shard_map/gather | solution.py:26
  97.7 2.1 reshape.46
  99.8 0.0 reduce-scatter.2.cloned.1.call-done
  99.8 0.0 copy-start.1
  99.8 2.0 fusion.1
  101.8 0.1 copy.12
  101.9 31.8 %psum.7 = f32[512,4]{0,1:T(4,128)S(1)} all-reduce(f32[512,4]{0,1:T(4,128)S(1)} %bitcast.23), channel_id=1, replica_groups=mesh['dp'=32,'wide'=16] {'wide'}, use_global_device_ids=true, to_apply=%region_1.0 | all-reduce | flops 2048 | bytes 16384 | tf_op jit(solution)/shard_map/psum | solution.py:30
  133.8 0.0 copy-done.1
  133.8 0.2 copy.13
  134.0 1.9 fusion.4
  135.9 0.7 fusion
  136.7 0.0 all-gather.5.cloned.1.call-update
  136.7 0.6 compare_select_fusion.1
  137.3 91.4 %all-gather.5.cloned.1.call-done = bf16[512,4096]{1,0:T(8,128)(2,1)} async-done(((bf16[512,256]{1,0:T(8,128)(2,1)}), bf16[512,4096]{1,0:T(8,128)(2,1)}) %all-gather.5.cloned.1.call-update) | async-done | bytes 4194320 | tf_op jit(solution)/shard_map/all_gather | solution.py:35
  228.7 4.9 %convolution_convert_fusion.1 = bf16[512,256]{1,0:T(8,128)(2,1)} fusion(bf16[512,4096]{1,0:T(8,128)(2,1)} %all-gather.5.cloned.1.call-done, bf16[256,4096]{1,0:T(8,128)(2,1)} %param.9, bf16[32,8,32,128]{3,2,1,0:T(8,128)(2,1)S(1)} %bitcast.22), kind=kOutput, calls=%fused_computation.3 | convolution fusion | flops 1074921472 | bytes 8650752 | tf_op jit(solution)/shard_map/dot_general | solution.py:36
  (3 shorter events, 0.0 us)
Async XLA Ops:
  8.0 1.8 copy-start
  8.0 76.7 %all-gather.3.cloned.1.call-start = ((), (), s32[]{:S(2)}) async-start(), calls=%async_computation.2 | async-start | bytes 8650752 | tf_op jit(solution)/shard_map/all_gather | solution.py:25
  8.7 91.1 %reduce-scatter.2.cloned.1.call-start = ((), (), s32[]{:S(2)}) async-start(), calls=%async_computation.1 | async-start | bytes 4456448 | tf_op jit(solution)/shard_map/reduce_scatter | solution.py:21
  15.7 0.7 copy-start.2
  15.7 213.0 %all-gather.5.cloned.1.call-start = ((), (), s32[]{:S(2)}) async-start(), calls=%async_computation.3 | async-start | bytes 4456448 | tf_op jit(solution)/shard_map/all_gather | solution.py:35
  99.8 33.9 %copy-start.1 = (s32[512,4]{0,1:T(4,128)S(1)}, s32[512,4]{0,1:T(4,128)}, u32[]{:S(2)}) copy-start(s32[512,4]{0,1:T(4,128)} %param.13) | copy-start | bytes 24580
Sparse Core Ops, SparseCore 0:
  12.0 72.6 all-gather.2
Sparse Core Ops, SparseCore 1:
  15.8 83.9 reduce-scatter.1
  136.8 91.9 all-gather.4
where the time goes:
time: 241 us
  waiting for transfers between devices  160 us (66%)
  blocking collectives  31.8 us (13%)
  local copies, waits for them, and re-layouts  16.8 us (7%)
  between operations  15.6 us (6%)
  matrix products  14.6 us (6%)
    all_gather x1, waiting for transfers between devices, local(): grad_full = lax.all_gather(grad_local, 'wide', axis=1, tiled=True)  91.4 us
    all_gather x1, waiting for transfers between devices, local(): whole = lax.all_gather(old_index, 'dp', axis=0, tiled=True)  67.9 us
    psum x1, blocking collectives, local(): score = lax.psum(partial_scores, 'wide') * scale  31.8 us
    gather x1, local copies, waits for them, and re-layouts, local(): old_vec = whole[flat].reshape(rows, K, e_local)  13 us
    dot_general x1, matrix products, local(): term = jnp.dot(query, masked, preferred_element_type=jnp.float32)  5.83 us
    dot_general x1, matrix products, local(): lax.dot_general(grad_full, masked, (((1,), (1,)), ((), ())), preferred_el...  4.9 us
  transfers between devices with their start and end apart: 3, of which 2 were waited for; matrix products, arithmetic and copies ran while one was open for 10% of the time, Pallas kernels for 0%

commit v1 on v0

--- a/solution.py
+++ b/solution.py
@@ -32,7 +32,12 @@
     pair_loss = jax.nn.softplus(-sign * score)
     dscore = -sign * jax.nn.sigmoid(-sign * score)
     grad_local = (jnp.einsum("rk,rke->re", dscore, old_wide) * scale).astype(jnp.bfloat16)
-    grad_full = lax.all_gather(grad_local, "wide", axis=1, tiled=True)
+    ring = [grad_local]
+    for hop in range(15):
+        ring.append(lax.ppermute(ring[-1], "wide", [(dev, (dev + 1) % 16) for dev in range(16)]))
+    grad_full = jnp.roll(
+        jnp.concatenate(ring[::-1], axis=1), (lax.axis_index("wide") + 1) * ring[0].shape[1], axis=1
+    )
     trunk_grad = lax.dot_general(
         grad_full, masked, (((1,), (1,)), ((), ())), preferred_element_type=jnp.float32
     )

time: 241 us -> 332 us (1.38)
  waiting for transfers between devices: 160 us -> 198 us
  starting transfers between devices: 0.13 us -> 28.9 us
  local copies, waits for them, and re-layouts: 16.8 us -> 41.6 us
    ppermute x0 -> x15, waiting for transfers between devices: none -> 128 us  [local(): lax.ppermute(ring[-1], 'wide', [(dev, (dev + 1) % 16) for dev in range(16)])]
    all_gather x1 -> x0, waiting for transfers between devices: 91.4 us -> none  [local(): grad_full = lax.all_gather(grad_local, 'wide', axis=1, tiled=True)]
    ppermute x0 -> x15, starting transfers between devices: none -> 28.8 us  [local(): lax.ppermute(ring[-1], 'wide', [(dev, (dev + 1) % 16) for dev in range(16)])]
    unnamed x7 -> x91, local copies, waits for them, and re-layouts: 0.78 us -> 25.6 us
  transfers between devices with their start and end apart: 3 -> 17, of which waited for: 2 -> 17; matrix products, arithmetic and copies ran while one was open for 10% -> 7% of each run, Pallas kernels for 0% -> 0%
where the time goes in v1:
time: 332 us; the launch traced here: 330 us
  waiting for transfers between devices  198 us (60%)
  local copies, waits for them, and re-layouts  41.6 us (13%)
  blocking collectives  31.5 us (9%)
  starting transfers between devices  28.9 us (9%)
  between operations  16.2 us (5%)
  matrix products  12.1 us (4%)
    ppermute x15, waiting for transfers between devices, local(): lax.ppermute(ring[-1], 'wide', [(dev, (dev + 1) % 16) for dev in range(16)])  128 us
    all_gather x1, waiting for transfers between devices, local(): whole = lax.all_gather(old_index, 'dp', axis=0, tiled=True)  68.5 us
    psum x1, blocking collectives, local(): score = lax.psum(partial_scores, 'wide') * scale  31.5 us
    ppermute x15, starting transfers between devices, local(): lax.ppermute(ring[-1], 'wide', [(dev, (dev + 1) % 16) for dev in range(16)])  28.8 us
    unnamed x91, local copies, waits for them, and re-layouts  25.6 us
    gather x1, local copies, waits for them, and re-layouts, local(): old_vec = whole[flat].reshape(rows, K, e_local)  13 us
  transfers between devices with their start and end apart: 17, of which 17 were waited for; matrix products, arithmetic and copies ran while one was open for 7% of the time, Pallas kernels for 0%

profile of v1, /device:TPU:2, one launch (start us, length us, event | category | flops | bytes accessed | tf_op | source)
XLA Modules:
  0.0 330.5 jit_solution(16902310288693455402)
XLA Ops:
  9.8 5.9 %convolution_convert_fusion = bf16[512,4096]{1,0:T(8,128)(2,1)} fusion(bf16[512,1024]{1,0:T(8,128)(2,1)S(1)} %copy-done, bf16[1024,256]{1,0:T(8,128)(2,1)} %param.8, bf16[256,4096]{1,0:T(8,128)(2,1)} %param.9, bf16[32,8,32,128]{3,2,1,0:T(8,128)(2,1)S(1)} %bitcast.24), kind=kOutput, calls=%fused_computation.1 | convolution fusion | flops 1345454080 | bytes 9961472 | tf_op jit(solution)/shard_map/dot_general | solution.py:20
  16.2 68.5 %all-gather.2.cloned.1.call-done = bf16[16384,256]{1,0:T(8,128)(2,1)} async-done(((bf16[512,256]{1,0:T(8,128)(2,1)}), bf16[16384,256]{1,0:T(8,128)(2,1)}) %all-gather.2.cloned.1.call-update) | async-done | bytes 8388624 | tf_op jit(solution)/shard_map/all_gather | solution.py:25
  84.7 13.0 %gather_fusion = bf16[2048,256]{1,0:T(8,128)(2,1)} fusion(bf16[16384,256]{1,0:T(8,128)(2,1)} %all-gather.2.cloned.1.call-done, s32[2048]{0:T(1024)S(1)} %broadcast_clamp_fusion), kind=kCustom, calls=%fused_computation | custom fusion | bytes 2105344 | tf_op jit(solution)/shard_map/gather | solution.py:26
  97.7 2.2 reshape.46
  100.1 2.0 fusion.6
  102.2 31.5 %psum.7 = f32[512,4]{0,1:T(4,128)S(1)} all-reduce(f32[512,4]{0,1:T(4,128)S(1)} %bitcast.26), channel_id=1, replica_groups=mesh['dp'=32,'wide'=16] {'wide'}, use_global_device_ids=true, to_apply=%region_1.0 | all-reduce | flops 2048 | bytes 16384 | tf_op jit(solution)/shard_map/psum | solution.py:30
  134.0 1.9 fusion.10
  136.7 2.1 collective-permute-start
  138.8 9.3 %collective-permute-done = bf16[512,256]{1,0:T(8,128)(2,1)S(1)} collective-permute-done((bf16[512,256]{1,0:T(8,128)(2,1)S(1)}, bf16[512,256]{1,0:T(8,128)(2,1)S(1)}, u32[]{:S(2)}, u32[]{:S(2)}) %collective-permute-start) | collective-permute-done | bytes 262176 | tf_op jit(solution)/shard_map/ppermute | solution.py:37
  148.0 1.9 collective-permute-start.1
  150.0 9.9 %collective-permute-done.1 = bf16[512,256]{1,0:T(8,128)(2,1)S(1)} collective-permute-done((bf16[512,256]{1,0:T(8,128)(2,1)S(1)}, bf16[512,256]{1,0:T(8,128)(2,1)S(1)}, u32[]{:S(2)}, u32[]{:S(2)}) %collective-permute-start.1) | collective-permute-done | bytes 262176 | tf_op jit(solution)/shard_map/ppermute | solution.py:37
  160.6 1.9 collective-permute-start.2
  162.5 9.7 %collective-permute-done.2 = bf16[512,256]{1,0:T(8,128)(2,1)S(1)} collective-permute-done((bf16[512,256]{1,0:T(8,128)(2,1)S(1)}, bf16[512,256]{1,0:T(8,128)(2,1)S(1)}, u32[]{:S(2)}, u32[]{:S(2)}) %collective-permute-start.2) | collective-permute-done | bytes 262176 | tf_op jit(solution)/shard_map/ppermute | solution.py:37
  172.8 1.9 collective-permute-start.3
  174.8 8.9 %collective-permute-done.3 = bf16[512,256]{1,0:T(8,128)(2,1)S(1)} collective-permute-done((bf16[512,256]{1,0:T(8,128)(2,1)S(1)}, bf16[512,256]{1,0:T(8,128)(2,1)S(1)}, u32[]{:S(2)}, u32[]{:S(2)}) %collective-permute-start.3) | collective-permute-done | bytes 262176 | tf_op jit(solution)/shard_map/ppermute | solution.py:37
  184.3 1.9 collective-permute-start.4
  186.2 8.0 %collective-permute-done.4 = bf16[512,256]{1,0:T(8,128)(2,1)S(1)} collective-permute-done((bf16[512,256]{1,0:T(8,128)(2,1)S(1)}, bf16[512,256]{1,0:T(8,128)(2,1)S(1)}, u32[]{:S(2)}, u32[]{:S(2)}) %collective-permute-start.4) | collective-permute-done | bytes 262176 | tf_op jit(solution)/shard_map/ppermute | solution.py:37
  194.9 1.9 collective-permute-start.5
  196.8 7.5 %collective-permute-done.5 = bf16[512,256]{1,0:T(8,128)(2,1)S(1)} collective-permute-done((bf16[512,256]{1,0:T(8,128)(2,1)S(1)}, bf16[512,256]{1,0:T(8,128)(2,1)S(1)}, u32[]{:S(2)}, u32[]{:S(2)}) %collective-permute-start.5) | collective-permute-done | bytes 262176 | tf_op jit(solution)/shard_map/ppermute | solution.py:37
  205.1 1.9 collective-permute-start.6
  207.0 7.5 %collective-permute-done.6 = bf16[512,256]{1,0:T(8,128)(2,1)S(1)} collective-permute-done((bf16[512,256]{1,0:T(8,128)(2,1)S(1)}, bf16[512,256]{1,0:T(8,128)(2,1)S(1)}, u32[]{:S(2)}, u32[]{:S(2)}) %collective-permute-start.6) | collective-permute-done | bytes 262176 | tf_op jit(solution)/shard_map/ppermute | solution.py:37
  217.1 7.5 %collective-permute-done.7 = bf16[512,256]{1,0:T(8,128)(2,1)S(1)} collective-permute-done((bf16[512,256]{1,0:T(8,128)(2,1)S(1)}, bf16[512,256]{1,0:T(8,128)(2,1)S(1)}, u32[]{:S(2)}, u32[]{:S(2)}) %collective-permute-start.7) | collective-permute-done | bytes 262176 | tf_op jit(solution)/shard_map/ppermute | solution.py:37
  227.3 8.1 %collective-permute-done.8 = bf16[512,256]{1,0:T(8,128)(2,1)S(1)} collective-permute-done((bf16[512,256]{1,0:T(8,128)(2,1)S(1)}, bf16[512,256]{1,0:T(8,128)(2,1)S(1)}, u32[]{:S(2)}, u32[]{:S(2)}) %collective-permute-start.8) | collective-permute-done | bytes 262176 | tf_op jit(solution)/shard_map/ppermute | solution.py:37
  238.0 9.2 %collective-permute-done.9 = bf16[512,256]{1,0:T(8,128)(2,1)S(1)} collective-permute-done((bf16[512,256]{1,0:T(8,128)(2,1)S(1)}, bf16[512,256]{1,0:T(8,128)(2,1)S(1)}, u32[]{:S(2)}, u32[]{:S(2)}) %collective-permute-start.9) | collective-permute-done | bytes 262176 | tf_op jit(solution)/shard_map/ppermute | solution.py:37
  249.8 10.3 %collective-permute-done.10 = bf16[512,256]{1,0:T(8,128)(2,1)S(1)} collective-permute-done((bf16[512,256]{1,0:T(8,128)(2,1)S(1)}, bf16[512,256]{1,0:T(8,128)(2,1)S(1)}, u32[]{:S(2)}, u32[]{:S(2)}) %collective-permute-start.10) | collective-permute-done | bytes 262176 | tf_op jit(solution)/shard_map/ppermute | solution.py:37
  262.8 9.5 %collective-permute-done.11 = bf16[512,256]{1,0:T(8,128)(2,1)S(1)} collective-permute-done((bf16[512,256]{1,0:T(8,128)(2,1)S(1)}, bf16[512,256]{1,0:T(8,128)(2,1)S(1)}, u32[]{:S(2)}, u32[]{:S(2)}) %collective-permute-start.11) | collective-permute-done | bytes 262176 | tf_op jit(solution)/shard_map/ppermute | solution.py:37
  274.9 8.2 %collective-permute-done.12 = bf16[512,256]{1,0:T(8,128)(2,1)S(1)} collective-permute-done((bf16[512,256]{1,0:T(8,128)(2,1)S(1)}, bf16[512,256]{1,0:T(8,128)(2,1)S(1)}, u32[]{:S(2)}, u32[]{:S(2)}) %collective-permute-start.12) | collective-permute-done | bytes 262176 | tf_op jit(solution)/shard_map/ppermute | solution.py:37
  283.8 1.9 collective-permute-start.13
  285.7 7.7 %collective-permute-done.13 = bf16[512,256]{1,0:T(8,128)(2,1)} collective-permute-done((bf16[512,256]{1,0:T(8,128)(2,1)S(1)}, bf16[512,256]{1,0:T(8,128)(2,1)}, u32[]{:S(2)}, u32[]{:S(2)}) %collective-permute-start.13) | collective-permute-done | bytes 262176 | tf_op jit(solution)/shard_map/ppermute | solution.py:37
  293.4 1.9 collective-permute-start.14
  296.1 7.1 %collective-permute-done.14 = bf16[512,256]{1,0:T(8,128)(2,1)} collective-permute-done((bf16[512,256]{1,0:T(8,128)(2,1)}, bf16[512,256]{1,0:T(8,128)(2,1)}, u32[]{:S(2)}, u32[]{:S(2)}) %collective-permute-start.14) | collective-permute-done | bytes 262176 | tf_op jit(solution)/shard_map/ppermute | solution.py:37
  320.8 2.3 fusion.2
  (114 shorter events, 41.5 us)
Async XLA Ops:
  8.0 76.7 %all-gather.2.cloned.1.call-start = ((), (), s32[]{:S(2)}) async-start(), calls=%async_computation.2 | async-start | bytes 8650752 | tf_op jit(solution)/shard_map/all_gather | solution.py:25
  8.8 91.3 %reduce-scatter.2.cloned.1.call-start = ((), (), s32[]{:S(2)}) async-start(), calls=%async_computation.1 | async-start | bytes 4456448 | tf_op jit(solution)/shard_map/reduce_scatter | solution.py:21
  15.8 118.0 %copy-start.28 = (s32[512,4]{0,1:T(4,128)S(1)}, s32[512,4]{0,1:T(4,128)}, u32[]{:S(2)}) copy-start(s32[512,4]{0,1:T(4,128)} %param.13) | copy-start | bytes 24580
  136.7 11.3 %collective-permute-start = (bf16[512,256]{1,0:T(8,128)(2,1)S(1)}, bf16[512,256]{1,0:T(8,128)(2,1)S(1)}, u32[]{:S(2)}, u32[]{:S(2)}) collective-permute-start(bf16[512,256]{1,0:T(8,128)(2,1)S(1)} %fusion.5), channel_id=1, source_target_pairs={{0,1},{1,2},{2,3},{3,4},{4,5},{5,6},{6,7},{7,8},{8,9},{9,10},{10,1... | collective-permute-start | bytes 786440 | tf_op jit(solution)/shard_map/ppermute | solution.py:37
  148.0 11.8 %collective-permute-start.1 = (bf16[512,256]{1,0:T(8,128)(2,1)S(1)}, bf16[512,256]{1,0:T(8,128)(2,1)S(1)}, u32[]{:S(2)}, u32[]{:S(2)}) collective-permute-start(bf16[512,256]{1,0:T(8,128)(2,1)S(1)} %collective-permute-done), channel_id=1, source_target_pairs={{0,1},{1,2},{2,3},{3,4},{4,5},{5,6},{6,7},{7,8},{8,9},{9,10},{10,1... | collective-permute-start | bytes 786440 | tf_op jit(solution)/shard_map/ppermute | solution.py:37
  160.6 11.6 %collective-permute-start.2 = (bf16[512,256]{1,0:T(8,128)(2,1)S(1)}, bf16[512,256]{1,0:T(8,128)(2,1)S(1)}, u32[]{:S(2)}, u32[]{:S(2)}) collective-permute-start(bf16[512,256]{1,0:T(8,128)(2,1)S(1)} %collective-permute-done.1), channel_id=1, source_target_pairs={{0,1},{1,2},{2,3},{3,4},{4,5},{5,6},{6,7},{7,8},{8,9},{9,10},{10,1... | collective-permute-start | bytes 786440 | tf_op jit(solution)/shard_map/ppermute | solution.py:37
  172.8 10.8 %collective-permute-start.3 = (bf16[512,256]{1,0:T(8,128)(2,1)S(1)}, bf16[512,256]{1,0:T(8,128)(2,1)S(1)}, u32[]{:S(2)}, u32[]{:S(2)}) collective-permute-start(bf16[512,256]{1,0:T(8,128)(2,1)S(1)} %collective-permute-done.2), channel_id=1, source_target_pairs={{0,1},{1,2},{2,3},{3,4},{4,5},{5,6},{6,7},{7,8},{8,9},{9,10},{10,1... | collective-permute-start | bytes 786440 | tf_op jit(solution)/shard_map/ppermute | solution.py:37
  184.3 9.9 %collective-permute-start.4 = (bf16[512,256]{1,0:T(8,128)(2,1)S(1)}, bf16[512,256]{1,0:T(8,128)(2,1)S(1)}, u32[]{:S(2)}, u32[]{:S(2)}) collective-permute-start(bf16[512,256]{1,0:T(8,128)(2,1)S(1)} %collective-permute-done.3), channel_id=1, source_target_pairs={{0,1},{1,2},{2,3},{3,4},{4,5},{5,6},{6,7},{7,8},{8,9},{9,10},{10,1... | collective-permute-start | bytes 786440 | tf_op jit(solution)/shard_map/ppermute | solution.py:37
  194.9 9.5 %collective-permute-start.5 = (bf16[512,256]{1,0:T(8,128)(2,1)S(1)}, bf16[512,256]{1,0:T(8,128)(2,1)S(1)}, u32[]{:S(2)}, u32[]{:S(2)}) collective-permute-start(bf16[512,256]{1,0:T(8,128)(2,1)S(1)} %collective-permute-done.4), channel_id=1, source_target_pairs={{0,1},{1,2},{2,3},{3,4},{4,5},{5,6},{6,7},{7,8},{8,9},{9,10},{10,1... | collective-permute-start | bytes 786440 | tf_op jit(solution)/shard_map/ppermute | solution.py:37
  205.1 9.5 %collective-permute-start.6 = (bf16[512,256]{1,0:T(8,128)(2,1)S(1)}, bf16[512,256]{1,0:T(8,128)(2,1)S(1)}, u32[]{:S(2)}, u32[]{:S(2)}) collective-permute-start(bf16[512,256]{1,0:T(8,128)(2,1)S(1)} %collective-permute-done.5), channel_id=1, source_target_pairs={{0,1},{1,2},{2,3},{3,4},{4,5},{5,6},{6,7},{7,8},{8,9},{9,10},{10,1... | collective-permute-start | bytes 786440 | tf_op jit(solution)/shard_map/ppermute | solution.py:37
  215.2 9.5 %collective-permute-start.7 = (bf16[512,256]{1,0:T(8,128)(2,1)S(1)}, bf16[512,256]{1,0:T(8,128)(2,1)S(1)}, u32[]{:S(2)}, u32[]{:S(2)}) collective-permute-start(bf16[512,256]{1,0:T(8,128)(2,1)S(1)} %collective-permute-done.6), channel_id=1, source_target_pairs={{0,1},{1,2},{2,3},{3,4},{4,5},{5,6},{6,7},{7,8},{8,9},{9,10},{10,1... | collective-permute-start | bytes 786440 | tf_op jit(solution)/shard_map/ppermute | solution.py:37
  225.4 10.0 %collective-permute-start.8 = (bf16[512,256]{1,0:T(8,128)(2,1)S(1)}, bf16[512,256]{1,0:T(8,128)(2,1)S(1)}, u32[]{:S(2)}, u32[]{:S(2)}) collective-permute-start(bf16[512,256]{1,0:T(8,128)(2,1)S(1)} %collective-permute-done.7), channel_id=1, source_target_pairs={{0,1},{1,2},{2,3},{3,4},{4,5},{5,6},{6,7},{7,8},{8,9},{9,10},{10,1... | collective-permute-start | bytes 786440 | tf_op jit(solution)/shard_map/ppermute | solution.py:37
  236.1 11.1 %collective-permute-start.9 = (bf16[512,256]{1,0:T(8,128)(2,1)S(1)}, bf16[512,256]{1,0:T(8,128)(2,1)S(1)}, u32[]{:S(2)}, u32[]{:S(2)}) collective-permute-start(bf16[512,256]{1,0:T(8,128)(2,1)S(1)} %collective-permute-done.8), channel_id=1, source_target_pairs={{0,1},{1,2},{2,3},{3,4},{4,5},{5,6},{6,7},{7,8},{8,9},{9,10},{10,1... | collective-permute-start | bytes 786440 | tf_op jit(solution)/shard_map/ppermute | solution.py:37
  247.9 12.2 %collective-permute-start.10 = (bf16[512,256]{1,0:T(8,128)(2,1)S(1)}, bf16[512,256]{1,0:T(8,128)(2,1)S(1)}, u32[]{:S(2)}, u32[]{:S(2)}) collective-permute-start(bf16[512,256]{1,0:T(8,128)(2,1)S(1)} %collective-permute-done.9), channel_id=1, source_target_pairs={{0,1},{1,2},{2,3},{3,4},{4,5},{5,6},{6,7},{7,8},{8,9},{9,10},{10,1... | collective-permute-start | bytes 786440 | tf_op jit(solution)/shard_map/ppermute | solution.py:37
  260.9 11.4 %collective-permute-start.11 = (bf16[512,256]{1,0:T(8,128)(2,1)S(1)}, bf16[512,256]{1,0:T(8,128)(2,1)S(1)}, u32[]{:S(2)}, u32[]{:S(2)}) collective-permute-start(bf16[512,256]{1,0:T(8,128)(2,1)S(1)} %collective-permute-done.10), channel_id=1, source_target_pairs={{0,1},{1,2},{2,3},{3,4},{4,5},{5,6},{6,7},{7,8},{8,9},{9,10},{10,1... | collective-permute-start | bytes 786440 | tf_op jit(solution)/shard_map/ppermute | solution.py:37
  273.0 10.1 %collective-permute-start.12 = (bf16[512,256]{1,0:T(8,128)(2,1)S(1)}, bf16[512,256]{1,0:T(8,128)(2,1)S(1)}, u32[]{:S(2)}, u32[]{:S(2)}) collective-permute-start(bf16[512,256]{1,0:T(8,128)(2,1)S(1)} %collective-permute-done.11), channel_id=1, source_target_pairs={{0,1},{1,2},{2,3},{3,4},{4,5},{5,6},{6,7},{7,8},{8,9},{9,10},{10,1... | collective-permute-start | bytes 786440 | tf_op jit(solution)/shard_map/ppermute | solution.py:37
  283.8 9.6 %collective-permute-start.13 = (bf16[512,256]{1,0:T(8,128)(2,1)S(1)}, bf16[512,256]{1,0:T(8,128)(2,1)}, u32[]{:S(2)}, u32[]{:S(2)}) collective-permute-start(bf16[512,256]{1,0:T(8,128)(2,1)S(1)} %collective-permute-done.12), channel_id=1, source_target_pairs={{0,1},{1,2},{2,3},{3,4},{4,5},{5,6},{6,7},{7,8},{8,9},{9,10},{10,1... | collective-permute-start | bytes 786440 | tf_op jit(solution)/shard_map/ppermute | solution.py:37
  293.4 9.8 %collective-permute-start.14 = (bf16[512,256]{1,0:T(8,128)(2,1)}, bf16[512,256]{1,0:T(8,128)(2,1)}, u32[]{:S(2)}, u32[]{:S(2)}) collective-permute-start(bf16[512,256]{1,0:T(8,128)(2,1)} %collective-permute-done.13), channel_id=1, source_target_pairs={{0,1},{1,2},{2,3},{3,4},{4,5},{5,6},{6,7},{7,8},{8,9},{9,10},{10,1... | collective-permute-start | bytes 786440 | tf_op jit(solution)/shard_map/ppermute | solution.py:37
  295.3 24.9 %copy-start.27 = (bf16[512,256]{1,0:T(8,128)(2,1)S(1)}, bf16[512,256]{1,0:T(8,128)(2,1)}, u32[]{:S(2)}) copy-start(bf16[512,256]{1,0:T(8,128)(2,1)} %copy-done.26) | copy-start | bytes 786436
  295.3 24.9 %copy-start.25 = (bf16[512,256]{1,0:T(8,128)(2,1)S(1)}, bf16[512,256]{1,0:T(8,128)(2,1)}, u32[]{:S(2)}) copy-start(bf16[512,256]{1,0:T(8,128)(2,1)} %copy-done.24) | copy-start | bytes 786436
  295.3 25.0 %copy-start.23 = (bf16[512,256]{1,0:T(8,128)(2,1)S(1)}, bf16[512,256]{1,0:T(8,128)(2,1)}, u32[]{:S(2)}) copy-start(bf16[512,256]{1,0:T(8,128)(2,1)} %copy-done.22) | copy-start | bytes 786436
  295.3 25.0 %copy-start.21 = (bf16[512,256]{1,0:T(8,128)(2,1)S(1)}, bf16[512,256]{1,0:T(8,128)(2,1)}, u32[]{:S(2)}) copy-start(bf16[512,256]{1,0:T(8,128)(2,1)} %copy-done.20) | copy-start | bytes 786436
  295.3 25.0 %copy-start.19 = (bf16[512,256]{1,0:T(8,128)(2,1)S(1)}, bf16[512,256]{1,0:T(8,128)(2,1)}, u32[]{:S(2)}) copy-start(bf16[512,256]{1,0:T(8,128)(2,1)} %copy-done.18) | copy-start | bytes 786436
  295.3 25.1 %copy-start.17 = (bf16[512,256]{1,0:T(8,128)(2,1)S(1)}, bf16[512,256]{1,0:T(8,128)(2,1)}, u32[]{:S(2)}) copy-start(bf16[512,256]{1,0:T(8,128)(2,1)} %copy-done.16) | copy-start | bytes 786436
  295.4 25.1 %copy-start.15 = (bf16[512,256]{1,0:T(8,128)(2,1)S(1)}, bf16[512,256]{1,0:T(8,128)(2,1)}, u32[]{:S(2)}) copy-start(bf16[512,256]{1,0:T(8,128)(2,1)} %copy-done.14) | copy-start | bytes 786436
  295.4 25.1 %copy-start.13 = (bf16[512,256]{1,0:T(8,128)(2,1)S(1)}, bf16[512,256]{1,0:T(8,128)(2,1)}, u32[]{:S(2)}) copy-start(bf16[512,256]{1,0:T(8,128)(2,1)} %copy-done.12) | copy-start | bytes 786436
  295.4 25.1 %copy-start.11 = (bf16[512,256]{1,0:T(8,128)(2,1)S(1)}, bf16[512,256]{1,0:T(8,128)(2,1)}, u32[]{:S(2)}) copy-start(bf16[512,256]{1,0:T(8,128)(2,1)} %copy-done.10) | copy-start | bytes 786436
  295.4 25.2 %copy-start.9 = (bf16[512,256]{1,0:T(8,128)(2,1)S(1)}, bf16[512,256]{1,0:T(8,128)(2,1)}, u32[]{:S(2)}) copy-start(bf16[512,256]{1,0:T(8,128)(2,1)} %copy-done.8) | copy-start | bytes 786436
  295.4 25.2 %copy-start.7 = (bf16[512,256]{1,0:T(8,128)(2,1)S(1)}, bf16[512,256]{1,0:T(8,128)(2,1)}, u32[]{:S(2)}) copy-start(bf16[512,256]{1,0:T(8,128)(2,1)} %copy-done.6) | copy-start | bytes 786436
  295.4 25.2 %copy-start.5 = (bf16[512,256]{1,0:T(8,128)(2,1)S(1)}, bf16[512,256]{1,0:T(8,128)(2,1)}, u32[]{:S(2)}) copy-start(bf16[512,256]{1,0:T(8,128)(2,1)} %copy-done.4) | copy-start | bytes 786436
  295.4 25.3 %copy-start.2 = (f32[512,1,256]{2,1,0:T(1,128)S(1)}, f32[512,1,256]{2,1,0:T(1,128)}, u32[]{:S(2)}) copy-start(f32[512,1,256]{2,1,0:T(1,128)} %copy-done.1) | copy-start | bytes 1572868
  304.1 16.7 %copy-start.3 = (bf16[256,4096]{1,0:T(8,128)(2,1)S(1)}, bf16[256,4096]{1,0:T(8,128)(2,1)}, u32[]{:S(2)}) copy-start(bf16[256,4096]{1,0:T(8,128)(2,1)} %param.9) | copy-start | bytes 6291460
  (15 other events, 18.9 us)
Sparse Core Ops, SparseCore 0:
  12.0 72.6 all-gather.1
Sparse Core Ops, SparseCore 1:
  15.8 84.2 reduce-scatter.1
